TPU v7x, 256 devices: a whole 4x4x8 slice. The times are simulated.
256 devices in a mesh: group: 32 (over z, y), tensor: 8 (over x, core).
Axes of the slice: x: 4, y: 4, z: 8, core: 2. Of those that a mesh axis runs over, the one named last changes fastest.
Arguments:
- query: bfloat16 [2, 1024, 2048], P(None, 'group', 'tensor'), may hold values from -80 to 80
- self_kv: bfloat16 [2, 1024, 2, 2048], P(None, 'group', None, 'tensor'), may hold values from -6 to 6
- kv_pages: bfloat16 [2, 1536, 16, 2, 2048], P(None, 'group', None, None, 'tensor'), may hold values from -6 to 6
- page_dest: int32 [1536, 1], replicated, may hold values from 0 to 31; in each aligned block of 48 rows (0 to 47, 48 to 95, ...) at most 3 rows name the same one
- page_request: int32 [1536], replicated, may hold values from 0 to 1
- score_len: int32 [64], P('group'), may hold values from 1 to 16
- out_proj: bfloat16 [2, 2048, 2048], P(None, 'tensor'), may hold values from -0.125 to 0.125
- residual: bfloat16 [2, 1024, 2048], P(None, ('group', 'tensor')), may hold values from -6 to 6
- norm_gain: float32 [2, 2048], replicated, may hold values from 0.5 to 40
- norm_bias: float32 [2, 2048], replicated, may hold values from -3 to 3
- vocab: bfloat16 [2, 2048, 196608], P(None, None, ('group', 'tensor')), may hold values from -0.3984375 to 0.3984375
- targets: int32 [1024], replicated, may hold values from 0 to 196607
Outputs:
- logprob: float32 [2, 1024], P(None, ('group', 'tensor'))
Inputs may be any that keep to these rules, and one draw needn't show every extreme that they name: `page_dest`: the 48 pages of each aligned block (pages held by one group) go to any one group at most 3 times; some block sends exactly 3 to some group.
All inputs are finite; a program needn't handle non-finite values.
Results may differ from a plain program's by a relative error of at most 0.00097.
Values may be sent and summed in bfloat16 or wider, within the bound.
No kernel may reach another device: no remote copies, remote signals or barrier semaphores. Data moves between devices by JAX's collectives and lax.ppermute only.
A program may use at most 128 MiB of HBM per device.

v0:
```python
import math
import jax
import jax.numpy as jnp
from jax import lax
from jax.sharding import PartitionSpec as P

HEADS = 16
HEAD_DIM = 128
REQ_GRP = 2
SCORE_LEN = 16
NEGATIVE = -1e30
EPSILON = 1e-05


def alibi_slopes(head_count):
    return jnp.exp2(-8.0 * jnp.arange(1, head_count + 1).astype(jnp.float32) / head_count)


def lse_combine(peak, total, chosen, axis):
    top = jnp.max(peak, axis=axis, keepdims=True)
    total = jnp.sum(total * jnp.exp(peak - top), axis=axis)
    return (jnp.squeeze(top, axis), total, jnp.sum(chosen, axis=axis))


def per_device(
    query,
    self_kv,
    kv_pages,
    page_dest,
    page_request,
    score_len,
    out_proj,
    residual,
    norm_gain,
    norm_bias,
    vocab,
    targets,
):
    groups = lax.axis_size("group")
    shards = lax.axis_size("tensor")
    group_id = lax.axis_index("group")
    tensor_id = lax.axis_index("tensor")
    tok_grp = query.shape[1]
    flat_width = query.shape[2]
    head_local = flat_width // HEAD_DIM
    per_owner = kv_pages.shape[1]
    page_len = kv_pages.shape[2]
    capacity = 2 * per_owner // groups
    destination = page_dest[:, 0]
    page_total = destination.shape[0]
    buffer = groups * capacity
    width = residual.shape[2]
    local = jnp.arange(per_owner, dtype=jnp.int32)
    earlier = local[None, :] < local[:, None]
    my_dest = lax.dynamic_slice_in_dim(destination, group_id * per_owner, per_owner)
    my_position = jnp.sum(
        ((my_dest[None, :] == my_dest[:, None]) & earlier).astype(jnp.int32), axis=1
    )
    out_slot = my_dest * capacity + my_position
    slots = jnp.arange(buffer, dtype=jnp.int32)
    send_hot = out_slot[None, :] == slots[:, None]
    send_from = jnp.sum(jnp.where(send_hot, local[None, :], 0), axis=1)
    outgoing = jnp.take(kv_pages, send_from, axis=1)
    incoming = lax.all_to_all(outgoing, "group", split_axis=1, concat_axis=1, tiled=True)
    pages = jnp.arange(page_total, dtype=jnp.int32)
    mine = destination == group_id
    mine_blocks = mine.reshape(groups, per_owner)
    rank_in_block = jnp.sum(
        (mine_blocks[:, None, :] & earlier[None]).astype(jnp.int32), axis=2
    ).reshape(-1)
    arrival = pages // per_owner * capacity + rank_in_block
    recv_hot = mine[None, :] & (arrival[None, :] == slots[:, None])
    is_valid = jnp.any(recv_hot, axis=1)
    slot_page = jnp.sum(jnp.where(recv_hot, pages[None, :], 0), axis=1)
    slot_request = jnp.sum(jnp.where(recv_hot, page_request[None, :], 0), axis=1)
    slot_rank = jnp.sum(
        (
            mine[None, :]
            & (page_request[None, :] == slot_request[:, None])
            & (pages[None, :] < slot_page[:, None])
        ).astype(jnp.int32),
        axis=1,
    )
    request_ids = jnp.arange(REQ_GRP, dtype=jnp.int32)
    totals = jnp.sum(
        (mine[None, :] & (page_request[None, :] == request_ids[:, None])).astype(jnp.int32), axis=1
    )
    slopes = lax.dynamic_slice_in_dim(alibi_slopes(HEADS), tensor_id * head_local, head_local)
    score_scale = 1.0 / math.sqrt(HEAD_DIM)
    queries = query.reshape(2, tok_grp, head_local, HEAD_DIM)
    own_keys = self_kv[:, :, 0].reshape(2, tok_grp, head_local, HEAD_DIM)
    own_values = self_kv[:, :, 1].reshape(2, tok_grp, head_local, HEAD_DIM)
    token_ids = jnp.arange(tok_grp, dtype=jnp.int32)
    token_request = token_ids // SCORE_LEN
    token_step = token_ids % SCORE_LEN
    own_distance = (token_step[:, None] - token_step[None, :]).astype(jnp.float32)
    own_scores = (
        jnp.einsum("mthd,mshd->mhts", queries, own_keys, preferred_element_type=jnp.float32)
        * score_scale
    )
    own_scores = own_scores - slopes[None, :, None, None] * own_distance[None, None]
    own_allowed = (
        (token_request[:, None] == token_request[None, :])
        & (token_step[None, :] <= token_step[:, None])
    )[None, None]
    own_scores = jnp.where(own_allowed, own_scores, NEGATIVE)
    own_top = jnp.max(own_scores, -1)
    key_data = incoming[:, :, :, 0].reshape(2, buffer * page_len, head_local, HEAD_DIM)
    values = incoming[:, :, :, 1].reshape(2, buffer * page_len, head_local, HEAD_DIM)
    key_request = jnp.repeat(jnp.where(is_valid, slot_request, -1), page_len)
    key_position = (
        slot_rank[:, None] * page_len + jnp.arange(page_len, dtype=jnp.int32)[None, :]
    ).reshape(-1)
    context = totals[token_request] * page_len
    distance = ((context + token_step)[:, None] - key_position[None, :]).astype(jnp.float32)
    scores = (
        jnp.einsum("mthd,mkhd->mhtk", queries, key_data, preferred_element_type=jnp.float32)
        * score_scale
    )
    scores = scores - slopes[None, :, None, None] * distance[None, None]
    allowed = (key_request[None, :] == token_request[:, None])[None, None]
    scores = jnp.where(allowed, scores, NEGATIVE)
    row_top = jnp.maximum(jnp.max(scores, -1), own_top)
    exp_terms = jnp.where(allowed, jnp.exp(scores - row_top[..., None]), 0.0)
    denominator = jnp.sum(exp_terms, -1)
    numerator = jnp.einsum(
        "mhtk,mkhd->mthd",
        exp_terms.astype(jnp.bfloat16),
        values,
        preferred_element_type=jnp.float32,
    )
    own_terms = jnp.where(own_allowed, jnp.exp(own_scores - row_top[..., None]), 0.0)
    denominator = denominator + jnp.sum(own_terms, -1)
    numerator = numerator + jnp.einsum(
        "mhts,mshd->mthd",
        own_terms.astype(jnp.bfloat16),
        own_values,
        preferred_element_type=jnp.float32,
    )
    attended = (
        (numerator / jnp.transpose(denominator, (0, 2, 1))[..., None])
        .reshape(2, tok_grp, flat_width)
        .astype(jnp.bfloat16)
    )
    rows_local = tok_grp // shards
    partial = jnp.einsum("mtk,mkd->tmd", attended, out_proj, preferred_element_type=jnp.float32)
    parts = lax.all_to_all(
        partial.reshape(shards, rows_local, 2, width), "tensor", 0, 0, tiled=True
    )
    mixed = jnp.sum(parts, axis=0)
    hidden = residual.astype(jnp.float32) + jnp.transpose(mixed, (1, 0, 2))
    row_mean = jnp.mean(hidden, axis=-1, keepdims=True)
    centered = hidden - row_mean
    variance = jnp.mean(centered * centered, axis=-1, keepdims=True)
    normed = (
        centered / jnp.sqrt(variance + EPSILON) * norm_gain[:, None, :] + norm_bias[:, None, :]
    ).astype(jnp.bfloat16)
    voc_local = vocab.shape[2]
    offset = (group_id * shards + tensor_id) * voc_local
    everyone = lax.all_gather(normed, ("group", "tensor"), axis=1, tiled=True)
    logits = jnp.einsum("mnd,mdv->mnv", everyone, vocab, preferred_element_type=jnp.float32)
    local_peak = jnp.max(logits, axis=2)
    local_total = jnp.sum(jnp.exp(logits - local_peak[..., None]), axis=2)
    wanted = targets - offset
    hit = jnp.arange(voc_local, dtype=jnp.int32)[None, None, :] == wanted[None, :, None]
    local_chosen = jnp.sum(jnp.where(hit, logits, 0.0), axis=2)
    stats = jnp.stack([local_peak, local_total, local_chosen]).reshape(
        3, 2, groups, shards, rows_local
    )
    stats = lax.all_to_all(stats, "tensor", 3, 3, tiled=True)
    peak, total, chosen = lse_combine(stats[0], stats[1], stats[2], 2)
    stats = lax.all_to_all(jnp.stack([peak, total, chosen]), "group", 2, 2, tiled=True)
    peak, total, chosen = lse_combine(stats[0], stats[1], stats[2], 1)
    mine_lp = chosen - (peak + jnp.log(total))
    local_ids = tensor_id * rows_local + jnp.arange(rows_local, dtype=jnp.int32)
    keep_token = local_ids % SCORE_LEN < score_len[local_ids // SCORE_LEN]
    return jnp.where(keep_token[None, :], mine_lp, 0.0)


def solution(mesh):
    in_specs = (
        P(None, "group", "tensor"),
        P(None, "group", None, "tensor"),
        P(None, "group", None, None, "tensor"),
        P(),
        P(),
        P("group"),
        P(None, "tensor", None),
        P(None, ("group", "tensor"), None),
        P(),
        P(),
        P(None, None, ("group", "tensor")),
        P(),
    )
    out_specs = P(None, ("group", "tensor"))
    return jax.shard_map(
        per_device, mesh=mesh, in_specs=in_specs, out_specs=out_specs, check_vma=False
    )
```

profile of v0, /device:TPU:1, one launch (start us, length us, event | category | flops | bytes accessed | tf_op | source)
XLA Modules:
  0.0 330.0 jit_solution(15946534215800585845)
XLA Ops:
  6.5 0.9 dynamic-slice_bitcast_fusion
  7.4 0.2 convert_reduce_fusion.2
  7.6 0.8 multiply_add_fusion
  8.4 0.1 select_reduce_fusion.3
  8.5 10.7 %gather_fusion.1 = bf16[96,2,16,2,256]{4,3,2,1,0:T(2,128)(2,1)} fusion(bf16[2,48,16,2,256]{4,3,2,1,0:T(2,128)(2,1)} %param.14, s32[1024]{0:T(1024)S(1)} %pad_clamp_fusion), kind=kCustom, calls=%fused_computation.1 | custom fusion | bytes 6291840 | tf_op jit(solution)/shard_map/jit(_take)/gather | solution.py:63
  19.2 6.4 %fusion.2 = bf16[2,96,16,2,256]{4,3,2,0,1:T(2,128)(2,1)} fusion(bf16[96,2,16,2,256]{4,3,2,1,0:T(2,128)(2,1)} %gather_fusion.1, pred[96]{0:T(512)(128)(4,1)S(1)} %compare_and_fusion.1), kind=kLoop, calls=%fused_computation.8 | loop fusion | flops 1572864 | bytes 6291552 | tf_op jit(solution)/shard_map/jit(_take)/select_n | solution.py:63
  25.6 12.3 %all-to-all-start = ((bf16[2,96,16,2,256]{4,3,2,0,1:T(2,128)(2,1)}), bf16[2,96,16,2,256]{4,3,2,0,1:T(2,128)(2,1)}, u32[]{:S(2)}, u32[]{:S(2)}) async-start(bf16[2,96,16,2,256]{4,3,2,0,1:T(2,128)(2,1)} %fusion.2), calls=%async_computation | async-start | bytes 6291456 | tf_op jit(solution)/shard_map/all_to_all | solution.py:64
  37.9 0.2 all-gather.2.cloned.1.call-start
  38.2 0.1 eq.156
  38.3 0.6 convert_reduce_fusion
  39.0 0.3 select_reduce_fusion.2
  39.3 0.3 convert_reduce_fusion.1
  39.6 0.1 iota_add_fusion
  39.7 0.1 add.233
  39.8 0.2 fusion.29
  40.1 0.1 eq.160
  40.2 0.1 dynamic_slice.10
  40.2 0.1 fusion.58
  40.4 0.6 fusion.74
  41.0 1.2 fusion.67
  42.2 0.3 slice_reduce_fusion
  42.5 0.1 compare_and_fusion
  42.7 0.2 fusion.76
  42.9 0.1 broadcast_compare_fusion
  43.0 0.1 subtract_convert_fusion
  43.1 0.1 broadcast_multiply_fusion
  43.2 65.1 %all-to-all-done = bf16[2,96,16,2,256]{4,3,2,0,1:T(2,128)(2,1)} async-done(((bf16[2,96,16,2,256]{4,3,2,0,1:T(2,128)(2,1)}), bf16[2,96,16,2,256]{4,3,2,0,1:T(2,128)(2,1)}, u32[]{:S(2)}, u32[]{:S(2)}) %all-to-all-start) | async-done | bytes 3145760 | tf_op jit(solution)/shard_map/all_to_all | solution.py:64
  108.2 9.8 %fusion.73 = (bf16[2,96,16,1,256]{4,3,2,0,1:T(2,128)(2,1)}, bf16[2,96,16,1,256]{4,3,2,0,1:T(2,128)(2,1)S(1)}) fusion(bf16[2,96,16,2,256]{4,3,2,0,1:T(2,128)(2,1)} %all-to-all-done), kind=kLoop, calls=%fused_computation.145 | loop fusion | bytes 6291456 | tf_op jit(solution)/shard_map/slice | solution.py:109
  118.1 1.6 copy.71
  119.7 3.5 %reshape_squeeze.13 = bf16[2,1536,2,128]{3,2,1,0:T(2,128)(2,1)} reshape(bf16[2,96,16,1,256]{4,2,1,0,3:T(8,128)(2,1)} %copy.71) | data formatting | bytes 3145728 | tf_op jit(solution)/shard_map/reshape;squeeze | solution.py:108
  123.2 2.3 fusion.75
  125.5 0.3 fusion.26
  125.9 0.2 convolution_bitcast_fusion.1
  126.1 1.6 copy.70
  127.7 3.5 %reshape_squeeze.12 = bf16[2,1536,2,128]{3,2,1,0:T(2,128)(2,1)} reshape(bf16[2,96,16,1,256]{4,2,1,0,3:T(8,128)(2,1)} %copy.70) | data formatting | bytes 3145728 | tf_op jit(solution)/shard_map/reshape;squeeze | solution.py:109
  131.2 1.9 fusion.23
  133.2 0.5 convolution_bitcast_fusion
  133.6 0.2 reshape.477
  133.8 16.4 %all_to_all.20 = f32[8,4,2,2048]{3,1,2,0:T(4,128)S(1)} all-to-all(f32[8,4,2,2048]{3,1,2,0:T(4,128)S(1)} %copy.80), channel_id=1, replica_groups=mesh['group'=32,'tensor'=8] {'tensor'}, dimensions={0} | all-to-all | bytes 1048576 | tf_op jit(solution)/shard_map/all_to_all | solution.py:147
  150.2 0.1 reduce_sum.174
  150.3 0.1 fusion.57
  150.4 0.2 multiply_reduce_fusion
  150.6 0.1 add_convert_fusion
  150.7 0.6 copy.81
  151.4 0.6 iota_compare_fusion
  152.0 114.4 %all-gather.2.cloned.1.call-done = bf16[2,1024,2048]{2,0,1:T(2,128)(2,1)} async-done(((bf16[2,4,2048]{2,0,1:T(2,128)(2,1)}), bf16[2,1024,2048]{2,0,1:T(2,128)(2,1)}) %all-gather.2.cloned.1.call-update) | async-done | bytes 8388624 | tf_op jit(solution)/shard_map/all_gather | solution.py:160
  266.4 23.1 %fusion.77 = (f32[2,1024]{1,0:T(2,128)S(1)}, f32[2,1024,768]{1,2,0:T(8,128)}) fusion(bf16[2,2048,768]{2,1,0:T(8,128)(2,1)} %param.22, bf16[2,1024,2048]{2,0,1:T(2,128)(2,1)} %all-gather.2.cloned.1.call-done), kind=kOutput, calls=%fused_computation.149 | convolution fusion | flops 6444021760 | bytes 20979712 | tf_op jit(solution)/shard_map/mnd,mdv->mnv/dot_general | solution.py:161
  289.5 0.3 stack.21
  289.8 3.6 %exponential_reduce_fusion = (f32[2,1024]{1,0:T(2,128)S(1)}, f32[2,1024]{1,0:T(2,128)S(1)}) fusion(f32[2,1024,768]{1,2,0:T(8,128)} %get-tuple-element.20, f32[2,1024]{1,0:T(2,128)S(1)} %get-tuple-element.19, pred[1024,768]{0,1:T(8,128)(4,1)S(1)} %iota_compare_fusion), kind=kLoop, calls=%fused_computation.5 | loop fusion | flops 6287360 | bytes 7102464 | tf_op jit(solution)/shard_map/reduce_sum | solution.py:163
  293.4 0.3 stack.22
  293.7 1.0 stack.23
  294.7 1.0 pad_maximum_fusion
  295.7 0.4 copy.84
  296.1 0.7 reshape.516
  296.8 4.3 %all-to-all-start.2 = ((f32[8,1,768]{2,1,0:T(1,128)}), f32[8,1,768]{2,1,0:T(1,128)S(1)}, u32[]{:S(2)}, u32[]{:S(2)}) async-start(f32[8,1,768]{2,1,0:T(1,128)} %reshape.516), calls=%async_computation.2 | async-start | bytes 49152 | tf_op jit(solution)/shard_map/all_to_all | solution.py:170
  301.1 0.6 gather_fusion
  301.8 4.0 %all-to-all-done.2 = f32[8,1,768]{2,1,0:T(1,128)S(1)} async-done(((f32[8,1,768]{2,1,0:T(1,128)}), f32[8,1,768]{2,1,0:T(1,128)S(1)}, u32[]{:S(2)}, u32[]{:S(2)}) %all-to-all-start.2) | async-done | bytes 24608 | tf_op jit(solution)/shard_map/all_to_all | solution.py:170
  305.8 0.5 broadcast.583
  306.3 0.7 reduce.11
  307.0 0.1 reshape.517
  307.2 0.7 copy.86
  308.0 5.4 %all-to-all-start.3 = ((f32[3,2,32,4]{3,1,0,2:T(2,128)}), f32[3,2,32,4]{3,1,0,2:T(2,128)S(1)}, u32[]{:S(2)}, u32[]{:S(2)}) async-start(f32[3,2,32,4]{3,1,0,2:T(2,128)} %copy.86), calls=%async_computation.3 | async-start | bytes 196608 | tf_op jit(solution)/shard_map/all_to_all | solution.py:172
  313.4 9.1 %all-to-all-done.3 = f32[3,2,32,4]{3,1,0,2:T(2,128)S(1)} async-done(((f32[3,2,32,4]{3,1,0,2:T(2,128)}), f32[3,2,32,4]{3,1,0,2:T(2,128)S(1)}, u32[]{:S(2)}, u32[]{:S(2)}) %all-to-all-start.3) | async-done | bytes 3104 | tf_op jit(solution)/shard_map/all_to_all | solution.py:172
  322.6 0.6 subtract_select_fusion
  (54 shorter events, 0.8 us)
Async XLA Ops:
  6.5 126.6 %copy-start = (bf16[2,256,2048]{2,1,0:T(8,128)(2,1)S(1)}, bf16[2,256,2048]{2,1,0:T(8,128)(2,1)}, u32[]{:S(2)}) copy-start(bf16[2,256,2048]{2,1,0:T(8,128)(2,1)} %param.18) | copy-start | bytes 6291460
  25.6 12.5 %copy-start.9 = (s32[1536,1]{0,1:T(1,128)S(1)}, s32[1536,1]{0,1:T(1,128)}, u32[]{:S(2)}) copy-start(s32[1536,1]{0,1:T(1,128)} %param.15) | copy-start | bytes 18436
  25.6 13.4 %copy-start.5 = (s32[1536]{0:T(1024)S(1)}, s32[1536]{0:T(1024)}, u32[]{:S(2)}) copy-start(s32[1536]{0:T(1024)} %param.16) | copy-start | bytes 18436
  25.6 16.6 %copy-start.4 = (bf16[2,32,2,256]{3,2,1,0:T(2,128)(2,1)S(1)}, bf16[2,32,2,256]{3,2,1,0:T(2,128)(2,1)}, u32[]{:S(2)}) copy-start(bf16[2,32,2,256]{3,2,1,0:T(2,128)(2,1)} %param.13) | copy-start | bytes 196612
  25.6 17.1 %copy-start.6 = (bf16[2,32,256]{2,1,0:T(8,128)(2,1)S(1)}, bf16[2,32,256]{2,1,0:T(8,128)(2,1)}, u32[]{:S(2)}) copy-start(bf16[2,32,256]{2,1,0:T(8,128)(2,1)} %param.12) | copy-start | bytes 98308
  25.6 82.6 %all-to-all-start = ((bf16[2,96,16,2,256]{4,3,2,0,1:T(2,128)(2,1)}), bf16[2,96,16,2,256]{4,3,2,0,1:T(2,128)(2,1)}, u32[]{:S(2)}, u32[]{:S(2)}) async-start(bf16[2,96,16,2,256]{4,3,2,0,1:T(2,128)(2,1)} %fusion.2), calls=%async_computation | async-start | bytes 6291456 | tf_op jit(solution)/shard_map/all_to_all | solution.py:64
  37.9 228.5 %all-gather.2.cloned.1.call-start = ((), (), s32[]{:S(2)}) async-start(), calls=%async_computation.4 | async-start | bytes 8421376 | tf_op jit(solution)/shard_map/all_gather | solution.py:160
  123.2 2.9 copy-start.2
  133.1 17.2 %copy-start.3 = (bf16[2,4,2048]{2,1,0:T(4,128)(2,1)S(1)}, bf16[2,4,2048]{2,1,0:T(4,128)(2,1)}, u32[]{:S(2)}) copy-start(bf16[2,4,2048]{2,1,0:T(4,128)(2,1)} %param.19) | copy-start | bytes 98308
  133.1 17.5 %copy-start.7 = (f32[2,2048]{1,0:T(2,128)S(1)}, f32[2,2048]{1,0:T(2,128)}, u32[]{:S(2)}) copy-start(f32[2,2048]{1,0:T(2,128)} %param.21) | copy-start | bytes 49156
  133.1 17.5 %copy-start.8 = (f32[2,2048]{1,0:T(2,128)S(1)}, f32[2,2048]{1,0:T(2,128)}, u32[]{:S(2)}) copy-start(f32[2,2048]{1,0:T(2,128)} %param.20) | copy-start | bytes 49156
  133.1 18.3 %copy-start.10 = (s32[1024]{0:T(1024)S(1)}, s32[1024]{0:T(1024)}, u32[]{:S(2)}) copy-start(s32[1024]{0:T(1024)} %param.23) | copy-start | bytes 12292
  293.4 7.7 %copy-start.1 = (s32[2]{0:T(128)S(1)}, s32[2]{0:T(128)}, u32[]{:S(2)}) copy-start(s32[2]{0:T(128)} %param.17) | copy-start | bytes 28
  296.8 9.0 %all-to-all-start.2 = ((f32[8,1,768]{2,1,0:T(1,128)}), f32[8,1,768]{2,1,0:T(1,128)S(1)}, u32[]{:S(2)}, u32[]{:S(2)}) async-start(f32[8,1,768]{2,1,0:T(1,128)} %reshape.516), calls=%async_computation.2 | async-start | bytes 49152 | tf_op jit(solution)/shard_map/all_to_all | solution.py:170
  308.0 14.5 %all-to-all-start.3 = ((f32[3,2,32,4]{3,1,0,2:T(2,128)}), f32[3,2,32,4]{3,1,0,2:T(2,128)S(1)}, u32[]{:S(2)}, u32[]{:S(2)}) async-start(f32[3,2,32,4]{3,1,0,2:T(2,128)} %copy.86), calls=%async_computation.3 | async-start | bytes 196608 | tf_op jit(solution)/shard_map/all_to_all | solution.py:172
Sparse Core Ops, SparseCore 0:
  151.5 114.8 all-gather.1
where the time goes:
time: 331 us; the launch traced here: 330 us
  waiting for transfers between devices  193 us (58%)
  local copies, waits for them, and re-layouts  38.5 us (12%)
  matrix products  28.1 us (8%)
  starting transfers between devices  22.2 us (7%)
  other arithmetic  18.5 us (6%)
  blocking collectives  16.4 us (5%)
  between operations  13.7 us (4%)
    all_gather x1, waiting for transfers between devices, per_device(): everyone = lax.all_gather(normed, ('group', 'tensor'), axis=1, tiled=True)  114 us
    all_to_all x1, waiting for transfers between devices, per_device(): lax.all_to_all(outgoing, 'group', split_axis=1, concat_axis=1, tiled=True)  65.1 us
    dot_general x1, matrix products, per_device(): jnp.einsum('mnd,mdv->mnv', everyone, vocab, preferred_element_type=jnp.fl...  23.1 us
    all_to_all x1, blocking collectives, per_device(): lax.all_to_all(partial.reshape(shards, rows_local, 2, width), 'tensor', 0...  16.4 us
    all_to_all x1, starting transfers between devices, per_device(): lax.all_to_all(outgoing, 'group', split_axis=1, concat_axis=1, tiled=True)  12.3 us
    slice x2, local copies, waits for them, and re-layouts, per_device(): incoming[:, :, :, 1].reshape(2, buffer * page_len, head_local, HEAD_DIM)  11.5 us
    gather x1, local copies, waits for them, and re-layouts, per_device(): outgoing = jnp.take(kv_pages, send_from, axis=1)  10.7 us
    all_to_all x1, waiting for transfers between devices, per_device(): lax.all_to_all(jnp.stack([peak, total, chosen]), 'group', 2, 2, tiled=True)  9.06 us
  transfers between devices with their start and end apart: 4, of which 4 were waited for; matrix products, arithmetic and copies ran while one was open for 2% of the time, Pallas kernels for 0%

commit v1 on v0

--- a/solution.py
+++ b/solution.py
@@ -157,7 +157,10 @@
     ).astype(jnp.bfloat16)
     voc_local = vocab.shape[2]
     offset = (group_id * shards + tensor_id) * voc_local
-    everyone = lax.all_gather(normed, ("group", "tensor"), axis=1, tiled=True)
+    peers = lax.axis_size(("group", "tensor"))
+    blocks = jnp.stack([normed for _ in range(peers)])
+    blocks = lax.all_to_all(blocks, ("group", "tensor"), split_axis=0, concat_axis=0)
+    everyone = jnp.concatenate(blocks, axis=1)
     logits = jnp.einsum("mnd,mdv->mnv", everyone, vocab, preferred_element_type=jnp.float32)
     local_peak = jnp.max(logits, axis=2)
     local_total = jnp.sum(jnp.exp(logits - local_peak[..., None]), axis=2)

time: 331 us -> 416 us (1.26)
  waiting for transfers between devices: 193 us -> 263 us
  local copies, waits for them, and re-layouts: 38.5 us -> 66.3 us
  between operations: 13.7 us -> 0.36 us
  matrix products: 28.1 us -> 17.8 us
  starting transfers between devices: 22.2 us -> 32.3 us
    all_to_all x0 -> x1, waiting for transfers between devices: none -> 185 us  [per_device(): lax.all_to_all(blocks, ('group', 'tensor'), split_axis=0, concat_axis=0)]
    all_gather x1 -> x0, waiting for transfers between devices: 114 us -> none  [per_device(): everyone = lax.all_gather(normed, ('group', 'tensor'), axis=1, tiled=True)]
    reshape x0 -> x2, local copies, waits for them, and re-layouts: none -> 20.9 us  [per_device(): everyone = jnp.concatenate(blocks, axis=1)]
    dot_general x1, matrix products: 23.1 us -> 12.9 us  [per_device(): jnp.einsum('mnd,mdv->mnv', everyone, vocab, preferred_element_type=jnp.fl...]
    all_to_all x0 -> x1, starting transfers between devices: none -> 9.15 us  [per_device(): lax.all_to_all(blocks, ('group', 'tensor'), split_axis=0, concat_axis=0)]
    another operation x0 -> x1, local copies, waits for them, and re-layouts: none -> 7.49 us  [per_device(): blocks = jnp.stack([normed for _ in range(peers)])]
  transfers between devices with their start and end apart: 4 -> 4, of which waited for: 4 -> 4; matrix products, arithmetic and copies ran while one was open for 2% -> 1% of each run, Pallas kernels for 0% -> 0%
where the time goes in v1:
time: 416 us; the launch traced here: 415 us
  waiting for transfers between devices  263 us (63%)
  local copies, waits for them, and re-layouts  66.3 us (16%)
  starting transfers between devices  32.3 us (8%)
  other arithmetic  18.6 us (4%)
  matrix products  17.8 us (4%)
  blocking collectives  16 us (4%)
    all_to_all x1, waiting for transfers between devices, per_device(): lax.all_to_all(blocks, ('group', 'tensor'), split_axis=0, concat_axis=0)  185 us
    all_to_all x1, waiting for transfers between devices, per_device(): lax.all_to_all(outgoing, 'group', split_axis=1, concat_axis=1, tiled=True)  65.5 us
    reshape x2, local copies, waits for them, and re-layouts, per_device(): everyone = jnp.concatenate(blocks, axis=1)  20.9 us
    all_to_all x1, blocking collectives, per_device(): lax.all_to_all(partial.reshape(shards, rows_local, 2, width), 'tensor', 0...  16 us
    dot_general x1, matrix products, per_device(): jnp.einsum('mnd,mdv->mnv', everyone, vocab, preferred_element_type=jnp.fl...  12.9 us
    all_to_all x1, starting transfers between devices, per_device(): lax.all_to_all(outgoing, 'group', split_axis=1, concat_axis=1, tiled=True)  12.5 us
    slice x2, local copies, waits for them, and re-layouts, per_device(): incoming[:, :, :, 1].reshape(2, buffer * page_len, head_local, HEAD_DIM)  11.5 us
    gather x1, local copies, waits for them, and re-layouts, per_device(): outgoing = jnp.take(kv_pages, send_from, axis=1)  10.7 us
  transfers between devices with their start and end apart: 4, of which 4 were waited for; matrix products, arithmetic and copies ran while one was open for 1% of the time, Pallas kernels for 0%

profile of v1, /device:TPU:1, one launch (start us, length us, event | category | flops | bytes accessed | tf_op | source)
XLA Modules:
  0.0 414.8 jit_solution(9609983666114317429)
XLA Ops:
  0.0 0.9 dynamic-slice_bitcast_fusion
  0.9 0.2 convert_reduce_fusion.2
  1.1 0.8 multiply_add_fusion
  1.8 0.1 select_reduce_fusion.3
  2.0 10.7 %gather_fusion.1 = bf16[96,2,16,2,256]{4,3,2,1,0:T(2,128)(2,1)} fusion(bf16[2,48,16,2,256]{4,3,2,1,0:T(2,128)(2,1)} %param.14, s32[1024]{0:T(1024)S(1)} %pad_clamp_fusion), kind=kCustom, calls=%fused_computation.1 | custom fusion | bytes 6291840 | tf_op jit(solution)/shard_map/jit(_take)/gather | solution.py:63
  12.7 6.4 %fusion = bf16[2,96,16,2,256]{4,3,2,0,1:T(2,128)(2,1)} fusion(bf16[96,2,16,2,256]{4,3,2,1,0:T(2,128)(2,1)} %gather_fusion.1, pred[96]{0:T(512)(128)(4,1)S(1)} %compare_and_fusion.1), kind=kLoop, calls=%fused_computation.6 | loop fusion | flops 1572864 | bytes 6291552 | tf_op jit(solution)/shard_map/jit(_take)/select_n | solution.py:63
  19.1 12.5 %all-to-all-start = ((bf16[2,96,16,2,256]{4,3,2,0,1:T(2,128)(2,1)}), bf16[2,96,16,2,256]{4,3,2,0,1:T(2,128)(2,1)}, u32[]{:S(2)}, u32[]{:S(2)}) async-start(bf16[2,96,16,2,256]{4,3,2,0,1:T(2,128)(2,1)} %fusion), calls=%async_computation | async-start | bytes 6291456 | tf_op jit(solution)/shard_map/all_to_all | solution.py:64
  31.6 0.1 eq.156
  31.7 0.6 convert_reduce_fusion
  32.5 0.3 select_reduce_fusion.2
  32.7 0.3 convert_reduce_fusion.1
  33.1 0.1 add.233
  33.2 0.2 fusion.27
  33.5 0.1 eq.160
  33.6 0.1 dynamic_slice.10
  33.7 0.1 fusion.56
  33.8 0.6 fusion.72
  34.4 1.2 fusion.65
  35.6 0.3 slice_reduce_fusion
  36.1 0.2 fusion.74
  36.3 0.1 broadcast_compare_fusion
  36.4 0.1 subtract_convert_fusion
  36.5 0.1 broadcast_multiply_fusion
  36.6 65.5 %all-to-all-done = bf16[2,96,16,2,256]{4,3,2,0,1:T(2,128)(2,1)} async-done(((bf16[2,96,16,2,256]{4,3,2,0,1:T(2,128)(2,1)}), bf16[2,96,16,2,256]{4,3,2,0,1:T(2,128)(2,1)}, u32[]{:S(2)}, u32[]{:S(2)}) %all-to-all-start) | async-done | bytes 3145760 | tf_op jit(solution)/shard_map/all_to_all | solution.py:64
  102.1 9.8 %fusion.71 = (bf16[2,96,16,1,256]{4,3,2,0,1:T(2,128)(2,1)}, bf16[2,96,16,1,256]{4,3,2,0,1:T(2,128)(2,1)S(1)}) fusion(bf16[2,96,16,2,256]{4,3,2,0,1:T(2,128)(2,1)} %all-to-all-done), kind=kLoop, calls=%fused_computation.143 | loop fusion | bytes 6291456 | tf_op jit(solution)/shard_map/slice | solution.py:109
  111.9 1.6 copy.49
  113.5 3.5 reshape_squeeze.13
  117.1 2.3 fusion.73
  119.4 0.3 fusion.24
  119.7 0.2 convolution_bitcast_fusion.1
  119.9 1.6 copy.48
  121.6 3.5 reshape_squeeze.12
  125.1 1.9 fusion.21
  127.0 0.5 convolution_bitcast_fusion
  127.4 0.2 reshape.485
  127.7 16.0 %all_to_all.25 = f32[8,4,2,2048]{3,1,2,0:T(4,128)S(1)} all-to-all(f32[8,4,2,2048]{3,1,2,0:T(4,128)S(1)} %copy.58), channel_id=1, replica_groups=mesh['group'=32,'tensor'=8] {'tensor'}, dimensions={0} | all-to-all | bytes 1048576 | tf_op jit(solution)/shard_map/all_to_all | solution.py:147
  143.6 0.1 reduce_sum.174
  143.7 0.1 fusion.55
  143.9 0.2 multiply_reduce_fusion
  144.1 0.1 add_convert_fusion
  144.2 7.5 %stack.16 = bf16[256,2,4,2048]{3,2,1,0:T(4,128)(2,1)} broadcast(bf16[2,4,2048]{2,1,0:T(4,128)(2,1)S(1)} %add_convert_fusion), dimensions={1,2,3} | broadcast | bytes 8421376 | tf_op jit(solution)/shard_map/stack | solution.py:161
  151.7 9.1 %all-to-all-start.2 = ((bf16[256,2,4,2048]{3,2,1,0:T(4,128)(2,1)}), bf16[256,2,4,2048]{3,2,1,0:T(4,128)(2,1)}, u32[]{:S(2)}, u32[]{:S(2)}) async-start(bf16[256,2,4,2048]{3,2,1,0:T(4,128)(2,1)} %stack.16), calls=%async_computation.2 | async-start | bytes 16777216 | tf_op jit(solution)/shard_map/all_to_all | solution.py:162
  160.9 0.6 iota_compare_fusion
  161.4 184.9 %all-to-all-done.2 = bf16[256,2,4,2048]{3,2,1,0:T(4,128)(2,1)} async-done(((bf16[256,2,4,2048]{3,2,1,0:T(4,128)(2,1)}), bf16[256,2,4,2048]{3,2,1,0:T(4,128)(2,1)}, u32[]{:S(2)}, u32[]{:S(2)}) %all-to-all-start.2) | async-done | bytes 8388640 | tf_op jit(solution)/shard_map/all_to_all | solution.py:162
  346.3 8.4 %copy.59 = bf16[2,256,4,2048]{3,2,1,0:T(4,128)(2,1)} copy(bf16[2,256,4,2048]{3,2,0,1:T(4,128)(2,1)} %bitcast.14) | data formatting | bytes 16777216 | tf_op jit(solution)/shard_map/reshape | solution.py:163
  354.7 12.5 %reshape.487 = bf16[2,1024,2048]{2,1,0:T(8,128)(2,1)} reshape(bf16[2,256,4,2048]{3,2,1,0:T(4,128)(2,1)} %copy.59) | data formatting | bytes 16777216 | tf_op jit(solution)/shard_map/reshape | solution.py:163
  367.2 12.9 %fusion.75 = (f32[2,1024]{1,0:T(2,128)S(1)}, f32[2,1024,768]{1,2,0:T(8,128)}) fusion(bf16[2,1024,2048]{2,1,0:T(8,128)(2,1)} %reshape.487, bf16[2,2048,768]{2,1,0:T(8,128)(2,1)} %param.22), kind=kOutput, calls=%fused_computation.147 | convolution fusion | flops 6444021760 | bytes 20979712 | tf_op jit(solution)/shard_map/mnd,mdv->mnv/dot_general | solution.py:164
  380.1 0.3 stack.17
  380.4 3.8 exponential_reduce_fusion
  384.1 0.3 stack.18
  384.4 1.0 stack.19
  385.4 1.0 pad_maximum_fusion
  386.4 0.4 copy.61
  386.8 0.7 reshape.526
  387.5 5.4 %all-to-all-start.3 = ((f32[8,1,768]{2,1,0:T(1,128)}), f32[8,1,768]{2,1,0:T(1,128)S(1)}, u32[]{:S(2)}, u32[]{:S(2)}) async-start(f32[8,1,768]{2,1,0:T(1,128)} %reshape.526), calls=%async_computation.3 | async-start | bytes 49152 | tf_op jit(solution)/shard_map/all_to_all | solution.py:173
  393.0 0.6 gather_fusion
  393.6 4.0 all-to-all-done.3
  397.6 0.5 broadcast.585
  398.2 0.7 reduce.11
  398.9 0.1 reshape.527
  399.1 0.7 copy.63
  399.8 5.2 %all-to-all-start.4 = ((f32[3,2,32,4]{3,1,0,2:T(2,128)}), f32[3,2,32,4]{3,1,0,2:T(2,128)S(1)}, u32[]{:S(2)}, u32[]{:S(2)}) async-start(f32[3,2,32,4]{3,1,0,2:T(2,128)} %copy.63), calls=%async_computation.4 | async-start | bytes 196608 | tf_op jit(solution)/shard_map/all_to_all | solution.py:175
  405.1 9.1 %all-to-all-done.4 = f32[3,2,32,4]{3,1,0,2:T(2,128)S(1)} async-done(((f32[3,2,32,4]{3,1,0,2:T(2,128)}), f32[3,2,32,4]{3,1,0,2:T(2,128)S(1)}, u32[]{:S(2)}, u32[]{:S(2)}) %all-to-all-start.4) | async-done | bytes 3104 | tf_op jit(solution)/shard_map/all_to_all | solution.py:175
  414.3 0.6 subtract_select_fusion
  (57 shorter events, 1.0 us)
Async XLA Ops:
  0.0 126.9 %copy-start = (bf16[2,256,2048]{2,1,0:T(8,128)(2,1)S(1)}, bf16[2,256,2048]{2,1,0:T(8,128)(2,1)}, u32[]{:S(2)}) copy-start(bf16[2,256,2048]{2,1,0:T(8,128)(2,1)} %param.18) | copy-start | bytes 6291460
  19.1 12.5 %copy-start.10 = (s32[1536,1]{0,1:T(1,128)S(1)}, s32[1536,1]{0,1:T(1,128)}, u32[]{:S(2)}) copy-start(s32[1536,1]{0,1:T(1,128)} %param.15) | copy-start | bytes 18436
  19.1 13.4 %copy-start.6 = (s32[1536]{0:T(1024)S(1)}, s32[1536]{0:T(1024)}, u32[]{:S(2)}) copy-start(s32[1536]{0:T(1024)} %param.16) | copy-start | bytes 18436
  19.1 16.5 %copy-start.5 = (bf16[2,32,2,256]{3,2,1,0:T(2,128)(2,1)S(1)}, bf16[2,32,2,256]{3,2,1,0:T(2,128)(2,1)}, u32[]{:S(2)}) copy-start(bf16[2,32,2,256]{3,2,1,0:T(2,128)(2,1)} %param.13) | copy-start | bytes 196612
  19.1 17.0 %copy-start.7 = (bf16[2,32,256]{2,1,0:T(8,128)(2,1)S(1)}, bf16[2,32,256]{2,1,0:T(8,128)(2,1)}, u32[]{:S(2)}) copy-start(bf16[2,32,256]{2,1,0:T(8,128)(2,1)} %param.12) | copy-start | bytes 98308
  19.1 83.0 %all-to-all-start = ((bf16[2,96,16,2,256]{4,3,2,0,1:T(2,128)(2,1)}), bf16[2,96,16,2,256]{4,3,2,0,1:T(2,128)(2,1)}, u32[]{:S(2)}, u32[]{:S(2)}) async-start(bf16[2,96,16,2,256]{4,3,2,0,1:T(2,128)(2,1)} %fusion), calls=%async_computation | async-start | bytes 6291456 | tf_op jit(solution)/shard_map/all_to_all | solution.py:64
  117.0 2.9 copy-start.3
  126.9 16.8 %copy-start.4 = (bf16[2,4,2048]{2,1,0:T(4,128)(2,1)S(1)}, bf16[2,4,2048]{2,1,0:T(4,128)(2,1)}, u32[]{:S(2)}) copy-start(bf16[2,4,2048]{2,1,0:T(4,128)(2,1)} %param.19) | copy-start | bytes 98308
  127.0 17.1 %copy-start.8 = (f32[2,2048]{1,0:T(2,128)S(1)}, f32[2,2048]{1,0:T(2,128)}, u32[]{:S(2)}) copy-start(f32[2,2048]{1,0:T(2,128)} %param.21) | copy-start | bytes 49156
  127.0 17.1 %copy-start.9 = (f32[2,2048]{1,0:T(2,128)S(1)}, f32[2,2048]{1,0:T(2,128)}, u32[]{:S(2)}) copy-start(f32[2,2048]{1,0:T(2,128)} %param.20) | copy-start | bytes 49156
  151.7 9.2 %copy-start.11 = (s32[1024]{0:T(1024)S(1)}, s32[1024]{0:T(1024)}, u32[]{:S(2)}) copy-start(s32[1024]{0:T(1024)} %param.23) | copy-start | bytes 12292
  151.7 194.7 %all-to-all-start.2 = ((bf16[256,2,4,2048]{3,2,1,0:T(4,128)(2,1)}), bf16[256,2,4,2048]{3,2,1,0:T(4,128)(2,1)}, u32[]{:S(2)}, u32[]{:S(2)}) async-start(bf16[256,2,4,2048]{3,2,1,0:T(4,128)(2,1)} %stack.16), calls=%async_computation.2 | async-start | bytes 16777216 | tf_op jit(solution)/shard_map/all_to_all | solution.py:162
  380.4 34.5 %copy-start.1 = (bf16[2,256,2048]{2,1,0:T(8,128)(2,1)S(1)}, bf16[2,256,2048]{2,1,0:T(8,128)(2,1)}, u32[]{:S(2)}) copy-start(bf16[2,256,2048]{2,1,0:T(8,128)(2,1)} %param.18) | copy-start | bytes 6291460
  384.1 8.8 %copy-start.2 = (s32[2]{0:T(128)S(1)}, s32[2]{0:T(128)}, u32[]{:S(2)}) copy-start(s32[2]{0:T(128)} %param.17) | copy-start | bytes 28
  387.5 10.1 %all-to-all-start.3 = ((f32[8,1,768]{2,1,0:T(1,128)}), f32[8,1,768]{2,1,0:T(1,128)S(1)}, u32[]{:S(2)}, u32[]{:S(2)}) async-start(f32[8,1,768]{2,1,0:T(1,128)} %reshape.526), calls=%async_computation.3 | async-start | bytes 49152 | tf_op jit(solution)/shard_map/all_to_all | solution.py:173
  399.8 14.3 %all-to-all-start.4 = ((f32[3,2,32,4]{3,1,0,2:T(2,128)}), f32[3,2,32,4]{3,1,0,2:T(2,128)S(1)}, u32[]{:S(2)}, u32[]{:S(2)}) async-start(f32[3,2,32,4]{3,1,0,2:T(2,128)} %copy.63), calls=%async_computation.4 | async-start | bytes 196608 | tf_op jit(solution)/shard_map/all_to_all | solution.py:175
